TPU v7x, 32 devices: a whole 2x2x4 slice. The times are simulated.
32 devices in a mesh: heads: 4 (over y, core), seq: 8 (over z, x).
Axes of the slice: x: 2, y: 2, z: 4, core: 2. Of those that a mesh axis runs over, the one named last changes fastest.
Arguments:
- hidden: bfloat16 [8, 256, 2048], P('seq', 'heads'), may hold values from -6 to 6
- norm_gain: bfloat16 [2048], replicated, may hold values from 0.099609375 to 1.8984375
- router_weight: bfloat16 [2048, 4], replicated, may hold values from -0.125 to 0.125
- att_experts: int32 [8, 256, 2], P('seq'), may hold values from 0 to 3, all different within a row
- q_weight: bfloat16 [4, 2048, 1024], P(None, None, 'heads'), may hold values from -0.125 to 0.125
- kv_weight: bfloat16 [2, 2048, 1024], P(None, None, 'heads'), may hold values from -0.125 to 0.125
- o_weight: bfloat16 [4, 1024, 2048], P(None, 'heads'), may hold values from -1 to 1
- kv_cache: bfloat16 [2, 128, 128, 1024], P(None, 'seq', None, 'heads'), may hold values from -200 to 200
- cached_blocks: int32 [8], replicated, may hold values from 1 to 32, 128 in all
- tail_trim: int32 [8], replicated, may hold values from 0 to 127
- block_pool: int32 [128], replicated, may hold values from 0 to 127, each once
Outputs:
- attn_out: bfloat16 [8, 256, 2048], P('seq', 'heads')
Inputs may be any that keep to these rules, and one draw needn't show every extreme that they name: `block_pool`: the cached_blocks sum to 128, so every block belongs to one request.
All inputs are finite; a program needn't handle non-finite values.
Results may differ from a plain program's by a relative error of at most 0.019.
The roundings to bfloat16 on the way count: a program that leaves them out, or rounds other values in their place, can miss the bound.
Values may be sent and summed in bfloat16 or wider, within the bound.
No kernel may reach another device: no remote copies, remote signals or barrier semaphores. Data moves between devices by JAX's collectives and lax.ppermute only.
A program may use at most 128 MiB of HBM per device.

v0:
```python
import functools
import numpy as np
import jax
import jax.numpy as jnp
from jax import lax
from jax.sharding import PartitionSpec as P

HD = 128
NEG_FILL = -1e30


def rotate(values, positions):
    half_dim = values.shape[-1] // 2
    inverse = 10000.0 ** (-2.0 * jnp.arange(half_dim, dtype=jnp.float32) / values.shape[-1])
    angles = positions.astype(jnp.float32)[:, None] * inverse[None, :]
    target = (values.shape[0],) + (1,) * (values.ndim - 2) + (half_dim,)
    cosine = jnp.cos(angles).reshape(target)
    sine_part = jnp.sin(angles).reshape(target)
    leading_part = values[..., :half_dim]
    trailing_part = values[..., half_dim:]
    return jnp.concatenate(
        [
            leading_part * cosine - trailing_part * sine_part,
            trailing_part * cosine + leading_part * sine_part,
        ],
        axis=-1,
    )


def normalize(rows, norm_gain):
    wide_rows = rows.astype(jnp.float32)
    scaled = wide_rows * lax.rsqrt(jnp.mean(wide_rows * wide_rows, axis=-1, keepdims=True) + 1e-05)
    return (scaled * norm_gain.astype(jnp.float32)).astype(jnp.bfloat16)


def route(normed, router_weight, chosen):
    logits = jnp.dot(normed, router_weight, preferred_element_type=jnp.float32)
    experts_all = router_weight.shape[1]
    onehot = (chosen[:, :, None] == jnp.arange(experts_all, dtype=jnp.int32)[None, None, :]).astype(
        jnp.float32
    )
    picked = jnp.sum(onehot * logits[:, None, :], axis=-1)
    return (onehot, jax.nn.softmax(picked, axis=-1))


def split_bf16(x):
    hi = lax.reduce_precision(x, exponent_bits=8, mantissa_bits=7)
    lo = lax.reduce_precision(x - hi, exponent_bits=8, mantissa_bits=7)
    return (hi, lo)


def seq_cycle(mesh):
    size = mesh.shape["seq"]
    plain = list(range(size))
    try:
        devices = np.moveaxis(np.asarray(mesh.devices), mesh.axis_names.index("seq"), -1)
        line = devices.reshape(-1, size)[0]
        coords = np.array([list(d.coords) for d in line])
    except Exception:
        return plain
    varying = [k for k in range(coords.shape[1]) if len(set(coords[:, k])) > 1]
    if len(varying) == 1:
        order = sorted(plain, key=lambda j: coords[j, varying[0]])
        return order[0::2] + order[1::2][::-1]
    if len(varying) != 2:
        return plain
    dim_a, dim_b = varying
    values_a = sorted(set(coords[:, dim_a]))
    values_b = sorted(set(coords[:, dim_b]))
    if len(values_a) % 2:
        dim_a, dim_b, values_a, values_b = (dim_b, dim_a, values_b, values_a)
    if len(values_a) % 2 or len(values_a) * len(values_b) != size:
        return plain
    at = {(coords[j, dim_a], coords[j, dim_b]): j for j in plain}
    cycle = [at[a, values_b[0]] for a in values_a]
    for row, a in enumerate(reversed(values_a)):
        columns = values_b[1:] if row % 2 == 0 else values_b[1:][::-1]
        cycle += [at[a, b] for b in columns]
    if sorted(cycle) != plain:
        return plain
    return cycle


def shift_all_gather(piece, axis_name):
    size = lax.axis_size(axis_name)
    rank = lax.axis_index(axis_name)
    by_offset = [piece] + [
        lax.ppermute(piece, axis_name, [(i, (i + s) % size) for i in range(size)])
        for s in range(1, size)
    ]
    by_offset = jnp.stack(by_offset[:1] + by_offset[1:][::-1], axis=0)
    return jnp.take(by_offset, (jnp.arange(size, dtype=jnp.int32) - rank) % size, axis=0)


def shift_reduce_scatter(rows, axis_name):
    size = lax.axis_size(axis_name)
    rank = lax.axis_index(axis_name)
    share = rows.shape[0] // size
    total = lax.dynamic_slice_in_dim(rows, rank * share, share, 0).astype(jnp.float32)
    for s in range(1, size):
        piece = lax.dynamic_slice_in_dim(rows, (rank + s) % size * share, share, 0)
        moved = lax.ppermute(piece, axis_name, [(i, (i + s) % size) for i in range(size)])
        total = total + moved.astype(jnp.float32)
    return total


def ring_all_gather(piece, axis_name, cycle):
    size = len(cycle)
    forward = [(cycle[i], cycle[(i + 1) % size]) for i in range(size)]
    backward = [(cycle[(i + 1) % size], cycle[i]) for i in range(size)]
    ahead = size // 2
    behind = size - 1 - ahead
    from_behind, from_ahead = ([], [])
    moving = piece
    for _ in range(ahead):
        moving = lax.ppermute(moving, axis_name, forward)
        from_behind.append(moving)
    moving = piece
    for _ in range(behind):
        moving = lax.ppermute(moving, axis_name, backward)
        from_ahead.append(moving)
    return jnp.stack([piece] + from_ahead + from_behind[::-1], axis=0)


def per_device(
    cycle,
    hidden,
    norm_gain,
    router_weight,
    att_experts,
    q_weight,
    kv_weight,
    o_weight,
    kv_cache,
    cached_blocks,
    tail_trim,
    block_pool,
):
    head_count = lax.axis_size("heads")
    seq_rank = lax.axis_index("seq")
    block_size = kv_cache.shape[2]
    local_blocks = kv_cache.shape[1]
    local_heads = q_weight.shape[2] // HD
    scale_q = HD ** (-0.5)
    normed = normalize(hidden[0], norm_gain)
    gathered = lax.all_gather(normed, "heads", axis=0, tiled=True)
    new_count = gathered.shape[0]
    chosen = att_experts[0]
    cached_len = cached_blocks * block_size - tail_trim
    positions = cached_len[seq_rank] + jnp.arange(new_count, dtype=jnp.int32)
    onehot, gates = route(gathered, router_weight, chosen)
    every_q = jnp.einsum("nd,edc->nec", gathered, q_weight, preferred_element_type=jnp.float32)
    chosen_q = jnp.sum(onehot[:, :, :, None] * every_q[:, None, :, :], axis=2).reshape(
        new_count, 2, local_heads, HD
    )
    queries = rotate(chosen_q, positions).astype(jnp.bfloat16)
    fresh = jnp.einsum("nd,sdc->snc", gathered, kv_weight, preferred_element_type=jnp.float32)
    new_keys = rotate(fresh[0].reshape(new_count, local_heads, HD), positions).astype(jnp.bfloat16)
    new_values = fresh[1].reshape(new_count, local_heads, HD).astype(jnp.bfloat16)
    ring_queries = ring_all_gather(queries, "seq", cycle)
    request_count = ring_queries.shape[0]
    ring_size = len(cycle)
    position_of = np.argsort(np.asarray(cycle))
    position = jnp.asarray(position_of, dtype=jnp.int32)[seq_rank]
    pool_size = block_pool.shape[0]
    global_ids = seq_rank * local_blocks + jnp.arange(local_blocks, dtype=jnp.int32)
    matches = block_pool[None, :] == global_ids[:, None]
    slot_of = jnp.sum(
        jnp.where(matches, jnp.arange(pool_size, dtype=jnp.int32)[None, :], 0), axis=1
    )
    starts = jnp.cumsum(cached_blocks) - cached_blocks
    owner = jnp.sum((starts[None, :] <= slot_of[:, None]).astype(jnp.int32), axis=1) - 1
    ordinal = slot_of - starts[owner]
    owns = owner[None, :] == jnp.arange(request_count, dtype=jnp.int32)[:, None]
    self_scores = (
        jnp.einsum("nkhc,thc->hnkt", queries, new_keys, preferred_element_type=jnp.float32)
        * scale_q
    )
    causal = (
        jnp.arange(new_count, dtype=jnp.int32)[None, :]
        <= jnp.arange(new_count, dtype=jnp.int32)[:, None]
    )
    self_scores = jnp.where(causal[None, :, None, :], self_scores, NEG_FILL)
    self_best = jnp.max(self_scores, axis=-1)
    self_weights = jnp.exp(self_scores - self_best[..., None])
    self_total = jnp.sum(self_weights, axis=-1)
    self_accum = jnp.einsum(
        "hnkt,thc->hnkc",
        self_weights.astype(jnp.bfloat16),
        new_values,
        preferred_element_type=jnp.float32,
    )
    ring_queries, self_best, self_total, self_accum = lax.optimization_barrier(
        (ring_queries, self_best, self_total, self_accum)
    )
    owner_offset = (jnp.asarray(position_of, dtype=jnp.int32)[owner] - position) % ring_size
    block_queries = jnp.take(ring_queries, owner_offset, axis=0)
    keys_here = kv_cache[0].reshape(local_blocks, block_size, local_heads, HD)
    values_here = kv_cache[1].reshape(local_blocks, block_size, local_heads, HD)
    scores = (
        jnp.einsum(
            "bnkhc,bthc->bhnkt", block_queries, keys_here, preferred_element_type=jnp.float32
        )
        * scale_q
    )
    key_pos = ordinal[:, None] * block_size + jnp.arange(block_size, dtype=jnp.int32)[None, :]
    key_ok = key_pos < cached_len[owner][:, None]
    scores = jnp.where(key_ok[:, None, None, None, :], scores, NEG_FILL)
    block_best = jnp.max(scores, axis=-1)
    request_best = jnp.max(
        jnp.where(owns[:, :, None, None, None], block_best[None], NEG_FILL), axis=1
    )
    best_hi, best_lo = split_bf16(request_best)
    request_ref = best_hi + best_lo
    weights = jnp.exp(scores - jnp.take(request_ref, owner, axis=0)[..., None])
    block_totals = jnp.sum(weights, axis=-1)
    block_accum = jnp.einsum(
        "bhnkt,bthc->bhnkc",
        weights.astype(jnp.bfloat16),
        values_here,
        preferred_element_type=jnp.float32,
    )
    owns_f = owns.astype(jnp.float32)
    accum = jnp.einsum("rb,bhnkc->rhnkc", owns_f, block_accum, precision=lax.Precision.HIGHEST)
    totals = jnp.einsum("rb,bhnk->rhnk", owns_f, block_totals, precision=lax.Precision.HIGHEST)
    totals_hi, totals_lo = split_bf16(totals)
    stats = jnp.stack([best_hi, best_lo, totals_hi, totals_lo], axis=1).astype(jnp.bfloat16)
    stat_rows = stats.size // (request_count * HD)
    payload = jnp.concatenate(
        [
            accum.astype(jnp.bfloat16).reshape(request_count, -1, HD),
            stats.reshape(request_count, stat_rows, HD),
        ],
        axis=1,
    )
    received = lax.all_to_all(payload, "seq", 0, 0, tiled=True)
    acc_rows = local_heads * new_count * 2
    sources = received.shape[0]
    part_accum = (
        received[:, :acc_rows].astype(jnp.float32).reshape(sources, local_heads, new_count, 2, HD)
    )
    part_stats = (
        received[:, acc_rows:].astype(jnp.float32).reshape(sources, 4, local_heads, new_count, 2)
    )
    part_best = part_stats[:, 0] + part_stats[:, 1]
    part_totals = part_stats[:, 2] + part_stats[:, 3]
    cache_best = jnp.max(part_best, axis=0)
    factor = jnp.exp(part_best - cache_best[None])
    cache_total = jnp.sum(part_totals * factor, axis=0)
    cache_accum = jnp.sum(part_accum * factor[..., None], axis=0)
    peak = jnp.maximum(cache_best, self_best)
    cache_share = jnp.exp(cache_best - peak)
    self_share = jnp.exp(self_best - peak)
    numerator = cache_accum * cache_share[..., None] + self_accum * self_share[..., None]
    denominator = cache_total * cache_share + self_total * self_share
    attended = jnp.transpose(
        (numerator / denominator[..., None]).astype(jnp.bfloat16), (1, 2, 0, 3)
    ).reshape(new_count, 2, local_heads * HD)
    rows_each = new_count // head_count
    output = jnp.zeros((rows_each * lax.axis_size("heads"), o_weight.shape[2]), jnp.float32)
    for expert in range(o_weight.shape[0]):
        weight_expert = jnp.sum(onehot[:, :, expert] * gates, axis=1)
        picked = jnp.where(
            chosen[:, 0:1] == expert,
            attended[:, 0],
            jnp.where(chosen[:, 1:2] == expert, attended[:, 1], jnp.zeros_like(attended[:, 0])),
        )
        output = output + weight_expert[:, None] * jnp.dot(
            picked, o_weight[expert], preferred_element_type=jnp.float32
        )
    summed = shift_reduce_scatter(output.astype(jnp.bfloat16), "heads")
    return summed[None].astype(jnp.bfloat16)


def solution(mesh):
    return jax.shard_map(
        functools.partial(per_device, tuple(seq_cycle(mesh))),
        mesh=mesh,
        in_specs=(
            P("seq", "heads", None),
            P(),
            P(),
            P("seq", None, None),
            P(None, None, "heads"),
            P(None, None, "heads"),
            P(None, "heads", None),
            P(None, "seq", None, "heads"),
            P(),
            P(),
            P(),
        ),
        out_specs=P("seq", "heads", None),
        check_vma=False,
    )
```

profile of v0, /device:TPU:0, one launch (start us, length us, event | category | flops | bytes accessed | tf_op | source)
XLA Modules:
  0.0 194.5 jit_solution(13304430576117952579)
XLA Ops:
  6.5 0.8 convert_element_type.89
  7.4 1.1 fusion.36
  8.5 1.8 fusion.38
  10.3 0.8 reduce-window.9
  11.2 0.7 bitcast_subtract_fusion.1
  11.8 0.8 select_reduce_fusion.1
  12.8 0.7 gather_fusion
  13.4 0.7 gather_fusion.1
  14.1 0.7 dynamic_slice.19
  14.8 0.7 gather_fusion.2
  15.4 0.7 dynamic_slice.18
  16.1 0.7 add_convert_fusion.3
  16.8 2.7 %fusion.126 = (bf16[1,16,128,256]{3,2,1,0:T(8,128)(2,1)}, bf16[1,16,128,256]{3,2,1,0:T(8,128)(2,1)S(1)}) fusion(bf16[2,16,128,256]{3,2,1,0:T(8,128)(2,1)} %param.20), kind=kLoop, calls=%fused_computation.220 | loop fusion | bytes 4194304 | tf_op jit(solution)/shard_map/slice | solution.py:199
  19.6 1.3 copy.264
  20.9 0.7 fusion.114
  22.2 1.6 copy.265
  25.0 1.2 compare_and_fusion
  26.4 1.2 multiply_cosine_fusion
  27.5 2.4 %all-gather.2.cloned.1.call-done = bf16[256,2048]{1,0:T(8,128)(2,1)} async-done(((bf16[64,2048]{1,0:T(8,128)(2,1)}), bf16[256,2048]{1,0:T(8,128)(2,1)}) %all-gather.2.cloned.1.call-update) | async-done | bytes 1048592 | tf_op jit(solution)/shard_map/all_gather | solution.py:146
  29.9 3.8 %fusion.28 = f32[256,4,256]{2,0,1:T(8,128)S(1)} fusion(bf16[4,2048,256]{2,1,0:T(8,128)(2,1)} %param.17, bf16[256,2048]{1,0:T(8,128)(2,1)} %all-gather.2.cloned.1.call-done), kind=kOutput, calls=%fused_computation.41 | convolution fusion | flops 1073741824 | bytes 6291456 | tf_op jit(solution)/shard_map/nd,edc->nec/dot_general | solution.py:152
  33.7 1.1 multiply_reduce_fusion.1
  34.8 2.1 %copy.211 = f32[256,2,256]{0,2,1:T(8,128)} copy(f32[256,2,256]{2,0,1:T(8,128)} %multiply_reduce_fusion.1) | data formatting | bytes 1048576 | tf_op jit(solution)/shard_map/reduce_sum | solution.py:153
  36.9 1.8 fusion.127
  38.6 1.9 copy.261
  40.6 1.0 copy.260
  41.6 1.4 subtract_convert_fusion
  43.1 0.7 copy-done.4
  43.8 0.8 pad_maximum_fusion.1
  44.6 1.5 collective-permute-start
  46.6 1.0 convolution_bitcast_fusion
  47.7 0.7 copy-done.9
  48.6 1.0 subtract_convert_fusion.1
  49.6 1.0 slice.236
  50.6 1.4 fusion.129
  52.0 2.6 %collective-permute-done.3 = bf16[256,2,2,128]{3,0,1,2:T(8,128)(2,1)} collective-permute-done((bf16[256,2,2,128]{3,0,1,2:T(8,128)(2,1)}, bf16[256,2,2,128]{3,0,1,2:T(8,128)(2,1)}, u32[]{:S(2)}, u32[]{:S(2)}) %collective-permute-start.3) | collective-permute-done | bytes 262176 | tf_op jit(solution)/shard_map/ppermute | solution.py:116
  55.1 1.2 fusion.39
  56.3 1.5 collective-permute-start.1
  57.9 4.1 %collective-permute-done.4 = bf16[256,2,2,128]{3,0,1,2:T(8,128)(2,1)S(1)} collective-permute-done((bf16[256,2,2,128]{3,0,1,2:T(8,128)(2,1)}, bf16[256,2,2,128]{3,0,1,2:T(8,128)(2,1)S(1)}, u32[]{:S(2)}, u32[]{:S(2)}) %collective-permute-start.4) | collective-permute-done | bytes 262176 | tf_op jit(solution)/shard_map/ppermute | solution.py:116
  62.8 0.7 collective-permute-done.1
  63.5 1.5 collective-permute-start.2
  65.0 1.0 bitcast_dynamic-update-slice_fusion.6
  66.0 2.8 %collective-permute-done.5 = bf16[256,2,2,128]{3,0,1,2:T(8,128)(2,1)S(1)} collective-permute-done((bf16[256,2,2,128]{3,0,1,2:T(8,128)(2,1)S(1)}, bf16[256,2,2,128]{3,0,1,2:T(8,128)(2,1)S(1)}, u32[]{:S(2)}, u32[]{:S(2)}) %collective-permute-start.5) | collective-permute-done | bytes 262176 | tf_op jit(solution)/shard_map/ppermute | solution.py:116
  69.9 5.2 %collective-permute-done.6 = bf16[256,2,2,128]{3,0,1,2:T(8,128)(2,1)S(1)} collective-permute-done((bf16[256,2,2,128]{3,0,1,2:T(8,128)(2,1)S(1)}, bf16[256,2,2,128]{3,0,1,2:T(8,128)(2,1)S(1)}, u32[]{:S(2)}, u32[]{:S(2)}) %collective-permute-start.6) | collective-permute-done | bytes 262176 | tf_op jit(solution)/shard_map/ppermute | solution.py:116
  75.3 1.0 bitcast_dynamic-update-slice_fusion
  76.3 3.2 %gather_fusion.3 = bf16[16,256,2,2,128]{4,1,2,3,0:T(8,128)(2,1)} fusion(bf16[8,256,2,2,128]{4,1,2,3,0:T(8,128)(2,1)S(1)} %bitcast_dynamic-update-slice_fusion, s32[1024]{0:T(1024)} %pad_clamp_fusion), kind=kCustom, calls=%fused_computation.3 | custom fusion | bytes 8388672 | tf_op jit(solution)/shard_map/jit(_take)/gather | solution.py:197
  79.5 8.0 %fusion.2 = (f32[16,2,256,2]{2,3,1,0:T(2,128)S(1)}, f32[16,2,256,2,128]{2,4,3,1,0:T(8,128)}) fusion(pred[16,128]{1,0:T(8,128)(4,1)S(1)} %add_compare_fusion, bf16[16,128,2,128,1]{1,3,4,2,0:T(8,128)(2,1)} %bitcast.182, bf16[16,256,2,2,128]{4,1,2,3,0:T(8,128)(2,1)} %gather_fusion.3, pred[16]{0:T(512)(128)(4,1)S(1)} %copy-done.18), kind=kOutput, calls=%fused_computation.9 | convolution fusion | flops 545243136 | bytes 13699088 | tf_op jit(solution)/shard_map/bnkhc,bthc->bhnkt/dot_general | solution.py:201
  87.8 0.7 gather_fusion.4
  88.6 4.7 %fusion.3 = f32[16,2,256,2]{2,3,1,0:T(2,128)S(1)} fusion(f32[16,2,256,2,128]{2,4,3,1,0:T(8,128)} %get-tuple-element.54, f32[16,2,256,2]{2,3,1,0:T(2,128)S(1)} %broadcast_select_fusion, pred[16,128]{1,0:T(8,128)(4,1)S(1)} %add_compare_fusion), kind=kLoop, calls=%fused_computation.10 | loop fusion | flops 8372224 | bytes 8521728 | tf_op jit(solution)/shard_map/reduce_sum | solution.py:216
  93.5 0.7 copy.231
  94.6 5.2 %fusion.5 = f32[16,2,256,2,128]{4,2,3,1,0:T(8,128)S(1)} fusion(bf16[16,128,2,128,1]{1,3,4,2,0:T(8,128)(2,1)S(1)} %bitcast.172, f32[16,2,256,2,128]{2,4,3,1,0:T(8,128)} %get-tuple-element.54, f32[16,2,256,2]{2,3,1,0:T(2,128)S(1)} %broadcast_select_fusion, pred[16,128]{1,0:T(8,128)(4,1)S(1)} %add_compare_fusion), kind=kOutput, calls=%fused_computation.12 | convolution fusion | flops 545259520 | bytes 17893376 | tf_op jit(solution)/shard_map/bhnkt,bthc->bhnkc/dot_general | solution.py:217
  99.8 6.3 %fusion.19 = bf16[8,2,256,2,128]{4,0,3,2,1:T(8,128)(2,1)S(1)} fusion(f32[16,2,256,2,128]{4,2,3,1,0:T(8,128)S(1)} %fusion.5, s32[16]{0:T(128)S(1)} %copy-done.16), kind=kOutput, calls=%fused_computation.32 | convolution fusion | flops 202375296 | bytes 10485824 | tf_op jit(solution)/shard_map/rb,bhnkc->rhnkc/dot_general | solution.py:224
  106.4 1.5 pad_maximum_fusion
  107.9 4.7 %all-to-all-start = ((bf16[8,1056,128]{2,1,0:T(8,128)(2,1)}), bf16[8,1056,128]{2,1,0:T(8,128)(2,1)}, u32[]{:S(2)}, u32[]{:S(2)}) async-start(bf16[8,1056,128]{2,1,0:T(8,128)(2,1)} %pad_maximum_fusion), calls=%async_computation | async-start | bytes 4325376 | tf_op jit(solution)/shard_map/all_to_all | solution.py:236
  113.2 45.3 %all-to-all-done = bf16[8,1056,128]{2,1,0:T(8,128)(2,1)} async-done(((bf16[8,1056,128]{2,1,0:T(8,128)(2,1)}), bf16[8,1056,128]{2,1,0:T(8,128)(2,1)}, u32[]{:S(2)}, u32[]{:S(2)}) %all-to-all-start) | async-done | bytes 2162720 | tf_op jit(solution)/shard_map/all_to_all | solution.py:236
  158.5 0.9 slice_convert_fusion.1
  160.9 1.3 fusion.43
  162.6 3.1 %multiply_reduce_fusion = f32[1024,128]{1,0:T(8,128)S(1)} fusion(bf16[8,1056,128]{2,1,0:T(8,128)(2,1)} %all-to-all-done, f32[8,1024]{1,0:T(8,128)S(1)} %subtract_exponential_fusion.2), kind=kLoop, calls=%fused_computation.13 | loop fusion | flops 3014656 | bytes 2654208 | tf_op jit(solution)/shard_map/reduce_sum | solution.py:250
  166.4 1.7 convolution_multiply_fusion.3
  168.1 1.9 fusion.16
  171.5 0.9 constant_dynamic-slice_fusion.1
  172.9 6.5 %collective-permute-done.9 = bf16[64,2048]{1,0:T(8,128)(2,1)} collective-permute-done((bf16[64,2048]{1,0:T(8,128)(2,1)}, bf16[64,2048]{1,0:T(8,128)(2,1)}, u32[]{:S(2)}, u32[]{:S(2)}) %collective-permute-start.9) | collective-permute-done | bytes 262176 | tf_op jit(solution)/shard_map/ppermute | solution.py:102
  179.4 5.4 %collective-permute-done.8 = bf16[64,2048]{1,0:T(8,128)(2,1)} collective-permute-done((bf16[64,2048]{1,0:T(8,128)(2,1)}, bf16[64,2048]{1,0:T(8,128)(2,1)}, u32[]{:S(2)}, u32[]{:S(2)}) %collective-permute-start.8) | collective-permute-done | bytes 262176 | tf_op jit(solution)/shard_map/ppermute | solution.py:102
  184.9 0.8 collective-permute-done.7
  185.7 1.9 fusion.49
  (100 shorter events, 11.8 us)
Async XLA Ops:
  6.5 40.1 %copy-start = (bf16[2,2048,256]{2,1,0:T(8,128)(2,1)S(1)}, bf16[2,2048,256]{2,1,0:T(8,128)(2,1)}, u32[]{:S(2)}) copy-start(bf16[2,2048,256]{2,1,0:T(8,128)(2,1)} %param.18) | copy-start | bytes 6291460
  6.5 8.2 %copy-start.2 = (s32[8]{0:T(128)S(1)}, s32[8]{0:T(128)}, u32[]{:S(2)}) copy-start(s32[8]{0:T(128)} %constant.127.clone) | copy-start | bytes 100
  6.5 9.6 %copy-start.11 = (s32[1,256,2]{1,2,0:T(2,128)S(1)}, s32[1,256,2]{1,2,0:T(2,128)}, u32[]{:S(2)}) copy-start(s32[1,256,2]{1,2,0:T(2,128)} %param.16) | copy-start | bytes 6148
  6.5 23.4 %all-gather.2.cloned.1.call-start = ((), (), s32[]{:S(2)}) async-start(), calls=%async_computation.1 | async-start | bytes 1310720 | tf_op jit(solution)/shard_map/all_gather | solution.py:146
  12.8 3.4 %copy-start.13 = (s32[1024]{0:T(1024)}, s32[1024]{0:T(1024)S(1)}, u32[]{:S(2)}) copy-start(s32[1024]{0:T(1024)S(1)} %pad_clamp_fusion.1) | copy-start | bytes 12292
  24.4 9.2 %copy-start.15 = (s32[16]{0:T(128)}, s32[16]{0:T(128)S(1)}, u32[]{:S(2)}) copy-start(s32[16]{0:T(128)S(1)} %broadcast_add_fusion) | copy-start | bytes 196
  41.6 5.0 %copy-start.7 = (bf16[256,2048]{1,0:T(8,128)(2,1)S(1)}, bf16[256,2048]{1,0:T(8,128)(2,1)}, u32[]{:S(2)}) copy-start(bf16[256,2048]{1,0:T(8,128)(2,1)} %all-gather.2.cloned.1.call-done) | copy-start | bytes 3145732
  43.0 0.7 copy-start.4
  44.6 11.7 %collective-permute-start = (bf16[256,2,2,128]{3,0,1,2:T(8,128)(2,1)}, bf16[256,2,2,128]{3,0,1,2:T(8,128)(2,1)}, u32[]{:S(2)}, u32[]{:S(2)}) collective-permute-start(bf16[256,2,2,128]{3,0,1,2:T(8,128)(2,1)} %pad_maximum_fusion.1), channel_id=1, source_target_pairs={{1,0},{3,1},{5,3},{7,5},{6,7},{4,6},{2,4},{0,2},{9,8},{11,9},{13,1... | collective-permute-start | bytes 786440 | tf_op jit(solution)/shard_map/ppermute | solution.py:120
  46.1 8.5 %collective-permute-start.3 = (bf16[256,2,2,128]{3,0,1,2:T(8,128)(2,1)}, bf16[256,2,2,128]{3,0,1,2:T(8,128)(2,1)}, u32[]{:S(2)}, u32[]{:S(2)}) collective-permute-start(bf16[256,2,2,128]{3,0,1,2:T(8,128)(2,1)} %pad_maximum_fusion.1), channel_id=1, source_target_pairs={{0,1},{1,3},{3,5},{5,7},{7,6},{6,4},{4,2},{2,0},{8,9},{9,11},{11,1... | collective-permute-start | bytes 786440 | tf_op jit(solution)/shard_map/ppermute | solution.py:116
  47.6 0.8 copy-start.9
  47.6 3.0 %copy-start.10 = (pred[256,256]{0,1:T(8,128)(4,1)S(1)}, pred[256,256]{0,1:T(8,128)(4,1)}, u32[]{:S(2)}) copy-start(pred[256,256]{0,1:T(8,128)(4,1)} %iota_compare_fusion) | copy-start | bytes 196612
  50.6 12.0 %copy-start.5 = (bf16[256,2,2,64]{3,0,1,2:T(8,128)(2,1)S(1)}, bf16[256,2,2,64]{3,0,1,2:T(8,128)(2,1)}, u32[]{:S(2)}) copy-start(bf16[256,2,2,64]{3,0,1,2:T(8,128)(2,1)} %copy-done.4) | copy-start | bytes 393220
  54.6 7.5 %collective-permute-start.4 = (bf16[256,2,2,128]{3,0,1,2:T(8,128)(2,1)}, bf16[256,2,2,128]{3,0,1,2:T(8,128)(2,1)S(1)}, u32[]{:S(2)}, u32[]{:S(2)}) collective-permute-start(bf16[256,2,2,128]{3,0,1,2:T(8,128)(2,1)} %collective-permute-done.3), channel_id=1, source_target_pairs={{0,1},{1,3},{3,5},{5,7},{7,6},{6,4},{4,2},{2,0},{8,9},{9,11},{11,1... | collective-permute-start | bytes 786440 | tf_op jit(solution)/shard_map/ppermute | solution.py:116
  56.3 7.2 %collective-permute-start.1 = (bf16[256,2,2,128]{3,0,1,2:T(8,128)(2,1)}, bf16[256,2,2,128]{3,0,1,2:T(8,128)(2,1)S(1)}, u32[]{:S(2)}, u32[]{:S(2)}) collective-permute-start(bf16[256,2,2,128]{3,0,1,2:T(8,128)(2,1)} %collective-permute-done), channel_id=1, source_target_pairs={{1,0},{3,1},{5,3},{7,5},{6,7},{4,6},{2,4},{0,2},{9,8},{11,9},{13,1... | collective-permute-start | bytes 786440 | tf_op jit(solution)/shard_map/ppermute | solution.py:120
  62.1 6.7 %collective-permute-start.5 = (bf16[256,2,2,128]{3,0,1,2:T(8,128)(2,1)S(1)}, bf16[256,2,2,128]{3,0,1,2:T(8,128)(2,1)S(1)}, u32[]{:S(2)}, u32[]{:S(2)}) collective-permute-start(bf16[256,2,2,128]{3,0,1,2:T(8,128)(2,1)S(1)} %collective-permute-done.4), channel_id=1, source_target_pairs={{0,1},{1,3},{3,5},{5,7},{7,6},{6,4},{4,2},{2,0},{8,9},{9,11},{11,1... | collective-permute-start | bytes 786440 | tf_op jit(solution)/shard_map/ppermute | solution.py:116
  63.5 6.4 %collective-permute-start.2 = (bf16[256,2,2,128]{3,0,1,2:T(8,128)(2,1)S(1)}, bf16[256,2,2,128]{3,0,1,2:T(8,128)(2,1)S(1)}, u32[]{:S(2)}, u32[]{:S(2)}) collective-permute-start(bf16[256,2,2,128]{3,0,1,2:T(8,128)(2,1)S(1)} %collective-permute-done.1), channel_id=1, source_target_pairs={{1,0},{3,1},{5,3},{7,5},{6,7},{4,6},{2,4},{0,2},{9,8},{11,9},{13,1... | collective-permute-start | bytes 786440 | tf_op jit(solution)/shard_map/ppermute | solution.py:120
  68.8 6.4 %collective-permute-start.6 = (bf16[256,2,2,128]{3,0,1,2:T(8,128)(2,1)S(1)}, bf16[256,2,2,128]{3,0,1,2:T(8,128)(2,1)S(1)}, u32[]{:S(2)}, u32[]{:S(2)}) collective-permute-start(bf16[256,2,2,128]{3,0,1,2:T(8,128)(2,1)S(1)} %collective-permute-done.5), channel_id=1, source_target_pairs={{0,1},{1,3},{3,5},{5,7},{7,6},{6,4},{4,2},{2,0},{8,9},{9,11},{11,1... | collective-permute-start | bytes 786440 | tf_op jit(solution)/shard_map/ppermute | solution.py:116
  76.3 3.2 %copy-start.18 = (pred[16]{0:T(512)(128)(4,1)S(1)}, pred[16]{0:T(512)(128)(4,1)}, u32[]{:S(2)}) copy-start(pred[16]{0:T(512)(128)(4,1)} %get-tuple-element.56) | copy-start | bytes 52
  79.5 8.0 %copy-start.17 = (pred[8,16]{1,0:T(8,128)(4,1)S(1)}, pred[8,16]{1,0:T(8,128)(4,1)}, u32[]{:S(2)}) copy-start(pred[8,16]{1,0:T(8,128)(4,1)} %iota_compare_fusion.2) | copy-start | bytes 388
  87.8 0.8 copy-start.14
  88.6 4.7 %copy-start.16 = (s32[16]{0:T(128)S(1)}, s32[16]{0:T(128)}, u32[]{:S(2)}) copy-start(s32[16]{0:T(128)} %copy-done.15) | copy-start | bytes 196
  107.9 4.8 %copy-start.8 = (bf16[256,2048]{1,0:T(8,128)(2,1)S(1)}, bf16[256,2048]{1,0:T(8,128)(2,1)}, u32[]{:S(2)}) copy-start(bf16[256,2048]{1,0:T(8,128)(2,1)} %all-gather.2.cloned.1.call-done) | copy-start | bytes 3145732
  107.9 4.8 %copy-start.12 = (bf16[2048,4]{0,1:T(4,128)(2,1)S(1)}, bf16[2048,4]{0,1:T(4,128)(2,1)}, u32[]{:S(2)}) copy-start(bf16[2048,4]{0,1:T(4,128)(2,1)} %param.15) | copy-start | bytes 49156
  107.9 50.6 %all-to-all-start = ((bf16[8,1056,128]{2,1,0:T(8,128)(2,1)}), bf16[8,1056,128]{2,1,0:T(8,128)(2,1)}, u32[]{:S(2)}, u32[]{:S(2)}) async-start(bf16[8,1056,128]{2,1,0:T(8,128)(2,1)} %pad_maximum_fusion), calls=%async_computation | async-start | bytes 4325376 | tf_op jit(solution)/shard_map/all_to_all | solution.py:236
  162.2 3.5 %copy-start.6 = (f32[2,256,2,128]{3,1,2,0:T(8,128)S(1)}, f32[2,256,2,128]{3,1,2,0:T(8,128)}, u32[]{:S(2)}) copy-start(f32[2,256,2,128]{3,1,2,0:T(8,128)} %fusion.39) | copy-start | bytes 1572868
  168.1 2.5 %copy-start.3 = (bf16[4,256,2048]{2,1,0:T(8,128)(2,1)S(1)}, bf16[4,256,2048]{2,1,0:T(8,128)(2,1)}, u32[]{:S(2)}) copy-start(bf16[4,256,2048]{2,1,0:T(8,128)(2,1)} %param.19) | copy-start | bytes 12582916
  171.1 16.6 %copy-start.1 = (bf16[2,2048,256]{2,1,0:T(8,128)(2,1)S(1)}, bf16[2,2048,256]{2,1,0:T(8,128)(2,1)}, u32[]{:S(2)}) copy-start(bf16[2,2048,256]{2,1,0:T(8,128)(2,1)} %param.18) | copy-start | bytes 6291460
  172.4 7.0 %collective-permute-start.9 = (bf16[64,2048]{1,0:T(8,128)(2,1)}, bf16[64,2048]{1,0:T(8,128)(2,1)}, u32[]{:S(2)}, u32[]{:S(2)}) collective-permute-start(bf16[64,2048]{1,0:T(8,128)(2,1)} %get-tuple-element.35), channel_id=1, source_target_pairs={{0,24},{8,0},{16,8},{24,16},{1,25},{9,1},{17,9},{25,17},{2,26},{10... | collective-permute-start | bytes 786440 | tf_op jit(solution)/shard_map/ppermute | solution.py:102
  172.4 12.5 %collective-permute-start.8 = (bf16[64,2048]{1,0:T(8,128)(2,1)}, bf16[64,2048]{1,0:T(8,128)(2,1)}, u32[]{:S(2)}, u32[]{:S(2)}) collective-permute-start(bf16[64,2048]{1,0:T(8,128)(2,1)} %get-tuple-element.36), channel_id=1, source_target_pairs={{0,16},{8,24},{16,0},{24,8},{1,17},{9,25},{17,1},{25,9},{2,18},{10... | collective-permute-start | bytes 786440 | tf_op jit(solution)/shard_map/ppermute | solution.py:102
  172.6 13.1 %collective-permute-start.7 = (bf16[64,2048]{1,0:T(8,128)(2,1)S(1)}, bf16[64,2048]{1,0:T(8,128)(2,1)}, u32[]{:S(2)}, u32[]{:S(2)}) collective-permute-start(bf16[64,2048]{1,0:T(8,128)(2,1)S(1)} %get-tuple-element.34), channel_id=1, source_target_pairs={{0,8},{8,16},{16,24},{24,0},{1,9},{9,17},{17,25},{25,1},{2,10},{10... | collective-permute-start | bytes 786440 | tf_op jit(solution)/shard_map/ppermute | solution.py:102
Sparse Core Ops, SparseCore 0:
  10.4 19.4 all-gather.1
where the time goes:
time: 195 us; the launch traced here: 194 us
  waiting for transfers between devices  76.4 us (39%)
  matrix products  31.8 us (16%)
  other arithmetic  31.7 us (16%)
  local copies, waits for them, and re-layouts  28.7 us (15%)
  between operations  14 us (7%)
  starting transfers between devices  11.9 us (6%)
    all_to_all x1, waiting for transfers between devices, per_device(): received = lax.all_to_all(payload, 'seq', 0, 0, tiled=True)  45.3 us
    ppermute x4, waiting for transfers between devices, ring_all_gather(): moving = lax.ppermute(moving, axis_name, forward)  14.7 us
    ppermute x3, waiting for transfers between devices, shift_reduce_scatter(): lax.ppermute(piece, axis_name, [(i, (i + s) % size) for i in range(size)])  12.8 us
    unnamed x50, local copies, waits for them, and re-layouts  9.4 us
    dot_general x1, matrix products, per_device(): jnp.einsum('bnkhc,bthc->bhnkt', block_queries, keys_here, preferred_eleme...  7.99 us
    dot_general x1, matrix products, per_device(): jnp.einsum('rb,bhnkc->rhnkc', owns_f, block_accum, precision=lax.Precisio...  6.32 us
    dot_general x1, matrix products, per_device(): jnp.einsum('bhnkt,bthc->bhnkc', weights.astype(jnp.bfloat16), values_here...  5.22 us
    all_to_all x1, starting transfers between devices, per_device(): received = lax.all_to_all(payload, 'seq', 0, 0, tiled=True)  4.72 us
  transfers between devices with their start and end apart: 12, of which 11 were waited for; matrix products, arithmetic and copies ran while one was open for 13% of the time, Pallas kernels for 0%

commit v1 on v0

--- a/solution.py
+++ b/solution.py
@@ -233,7 +233,21 @@
         ],
         axis=1,
     )
-    received = lax.all_to_all(payload, "seq", 0, 0, tiled=True)
+    all_values = lax.axis_index("seq")
+    response = lax.axis_size("seq")
+    local_out, x_new = (response, all_values)
+    local_now = payload.shape[0] // local_out
+    piece_out = jnp.roll(payload, -x_new * local_now, axis=0)
+    e_now = lax.slice_in_dim(piece_out, 0, local_now, axis=0)
+    trail = [e_now]
+    for dev in range(1, local_out):
+        a_next = lax.slice_in_dim(piece_out, dev * local_now, (dev + 1) * local_now, axis=0)
+        trail.append(
+            lax.ppermute(a_next, "seq", [(h, (h + dev) % local_out) for h in range(local_out)])
+        )
+    received = jnp.roll(
+        jnp.concatenate(trail[::-1], axis=0), (x_new + 1) * trail[0].shape[0], axis=0
+    )
     acc_rows = local_heads * new_count * 2
     sources = received.shape[0]
     part_accum = (

time: 195 us -> 197 us (1.010)
  waiting for transfers between devices: 76.4 us -> 53.8 us
  starting transfers between devices: 11.9 us -> 33.6 us
  other arithmetic: 31.7 us -> 35.1 us
  local copies, waits for them, and re-layouts: 28.7 us -> 25.7 us
    all_to_all x1 -> x0, waiting for transfers between devices: 45.3 us -> none  [per_device(): received = lax.all_to_all(payload, 'seq', 0, 0, tiled=True)]
    ppermute x0 -> x7, starting transfers between devices: none -> 24.2 us  [per_device(): lax.ppermute(a_next, 'seq', [(h, (h + dev) % local_out) for h in range(lo...]
    ppermute x0 -> x7, waiting for transfers between devices: none -> 22.8 us  [per_device(): lax.ppermute(a_next, 'seq', [(h, (h + dev) % local_out) for h in range(lo...]
    concatenate x1 -> x2, other arithmetic: 1.47 us -> 9.05 us  [the longest x1 8.27 us: per_device(): piece_out = jnp.roll(payload, -x_new * local_now, axis=0)]
    all_to_all x1 -> x0, starting transfers between devices: 4.72 us -> none  [per_device(): received = lax.all_to_all(payload, 'seq', 0, 0, tiled=True)]
    ppermute x4, starting transfers between devices: 2.16 us -> 5.87 us  [ring_all_gather(): moving = lax.ppermute(moving, axis_name, forward)]
    ppermute x3, starting transfers between devices: 4.46 us -> 1.77 us  [ring_all_gather(): moving = lax.ppermute(moving, axis_name, backward)]
    another operation x4, other arithmetic: 3.27 us -> 1.06 us
  transfers between devices with their start and end apart: 12 -> 18, of which waited for: 11 -> 10; matrix products, arithmetic and copies ran while one was open for 13% -> 12% of each run, Pallas kernels for 0% -> 0%
where the time goes in v1:
time: 197 us; the launch traced here: 196 us
  waiting for transfers between devices  53.8 us (27%)
  other arithmetic  35.1 us (18%)
  starting transfers between devices  33.6 us (17%)
  matrix products  33.6 us (17%)
  local copies, waits for them, and re-layouts  25.7 us (13%)
  between operations  14.3 us (7%)
    ppermute x7, starting transfers between devices, per_device(): lax.ppermute(a_next, 'seq', [(h, (h + dev) % local_out) for h in range(lo...  24.2 us
    ppermute x7, waiting for transfers between devices, per_device(): lax.ppermute(a_next, 'seq', [(h, (h + dev) % local_out) for h in range(lo...  22.8 us
    ppermute x4, waiting for transfers between devices, ring_all_gather(): moving = lax.ppermute(moving, axis_name, forward)  16.3 us
    ppermute x3, waiting for transfers between devices, shift_reduce_scatter(): lax.ppermute(piece, axis_name, [(i, (i + s) % size) for i in range(size)])  12.8 us
    unnamed x77, local copies, waits for them, and re-layouts  8.83 us
    concatenate x1, other arithmetic, per_device(): piece_out = jnp.roll(payload, -x_new * local_now, axis=0)  8.27 us
    dot_general x1, matrix products, per_device(): jnp.einsum('bnkhc,bthc->bhnkt', block_queries, keys_here, preferred_eleme...  7.99 us
    dot_general x1, matrix products, per_device(): jnp.einsum('rb,bhnkc->rhnkc', owns_f, block_accum, precision=lax.Precisio...  6.31 us
  transfers between devices with their start and end apart: 18, of which 10 were waited for; matrix products, arithmetic and copies ran while one was open for 12% of the time, Pallas kernels for 0%

profile of v1, /device:TPU:0, one launch (start us, length us, event | category | flops | bytes accessed | tf_op | source)
XLA Modules:
  0.0 196.0 jit_solution(13481133562619845250)
XLA Ops:
  6.5 1.3 fusion.40
  7.8 0.7 convert_element_type.89
  8.5 1.8 fusion.42
  10.4 0.8 reduce-window.9
  11.2 0.8 select_reduce_fusion.1
  12.1 0.7 bitcast_subtract_fusion.1
  12.9 0.7 gather_fusion
  13.5 0.7 gather_fusion.1
  14.2 0.7 dynamic_slice.22
  15.4 0.7 gather_fusion.2
  18.6 2.8 %fusion.131 = (bf16[1,16,128,256]{3,2,1,0:T(8,128)(2,1)S(1)}, bf16[1,16,128,256]{3,2,1,0:T(8,128)(2,1)}) fusion(bf16[2,16,128,256]{3,2,1,0:T(8,128)(2,1)} %param.22), kind=kLoop, calls=%fused_computation.238 | loop fusion | bytes 4194304 | tf_op jit(solution)/shard_map/slice | solution.py:198
  21.4 1.4 copy.264
  22.8 1.6 copy.265
  24.4 0.6 iota_compare_fusion
  25.7 1.2 compare_and_fusion
  27.0 1.2 multiply_cosine_fusion
  28.1 1.8 all-gather.2.cloned.1.call-done
  30.0 2.2 %convolution_bitcast_fusion = f32[2,256,256]{1,2,0:T(8,128)S(1)} fusion(bf16[2,2048,256]{2,1,0:T(8,128)(2,1)S(1)} %copy-done, bf16[256,2048]{1,0:T(8,128)(2,1)} %all-gather.2.cloned.1.call-done), kind=kOutput, calls=%fused_computation.44 | convolution fusion | flops 536870912 | bytes 3670016 | tf_op jit(solution)/shard_map/nd,sdc->snc/dot_general | solution.py:157
  32.2 0.7 slice.277
  32.9 3.5 %fusion.32 = f32[256,4,256]{2,0,1:T(8,128)S(1)} fusion(bf16[4,2048,256]{2,1,0:T(8,128)(2,1)} %param.19, bf16[256,2048]{1,0:T(8,128)(2,1)S(1)} %copy-done.10), kind=kOutput, calls=%fused_computation.50 | convolution fusion | flops 1073741824 | bytes 6291456 | tf_op jit(solution)/shard_map/nd,edc->nec/dot_general | solution.py:152
  38.0 1.5 collective-permute-start.3
  40.4 1.3 fusion.134
  41.7 2.1 %fusion.43 = f32[2,256,2,128]{3,1,2,0:T(8,128)} fusion(bf16[256,2,128,1]{0,2,3,1:T(8,128)(2,1)} %bitcast.184, f32[2,256,2,256]{1,3,2,0:T(8,128)S(1)} %get-tuple-element.60, f32[2,256,2]{1,2,0:T(2,128)S(1)} %get-tuple-element.11), kind=kOutput, calls=%fused_computation.64 | convolution fusion | flops 67633152 | bytes 1708032 | tf_op jit(solution)/shard_map/hnkt,thc->hnkc/dot_general | solution.py:187
  43.8 2.7 %collective-permute-done.3 = bf16[256,2,2,128]{3,0,1,2:T(8,128)(2,1)} collective-permute-done((bf16[256,2,2,128]{3,0,1,2:T(8,128)(2,1)S(1)}, bf16[256,2,2,128]{3,0,1,2:T(8,128)(2,1)}, u32[]{:S(2)}, u32[]{:S(2)}) %collective-permute-start.3) | collective-permute-done | bytes 262176 | tf_op jit(solution)/shard_map/ppermute | solution.py:116
  46.6 1.5 collective-permute-start.4
  49.2 5.3 %collective-permute-done.4 = bf16[256,2,2,128]{3,0,1,2:T(8,128)(2,1)S(1)} collective-permute-done((bf16[256,2,2,128]{3,0,1,2:T(8,128)(2,1)}, bf16[256,2,2,128]{3,0,1,2:T(8,128)(2,1)S(1)}, u32[]{:S(2)}, u32[]{:S(2)}) %collective-permute-start.4) | collective-permute-done | bytes 262176 | tf_op jit(solution)/shard_map/ppermute | solution.py:116
  54.4 1.4 collective-permute-start.5
  56.0 0.6 collective-permute-start.2
  56.7 1.0 bitcast_dynamic-update-slice_fusion.6
  57.7 3.5 %collective-permute-done.5 = bf16[256,2,2,128]{3,0,1,2:T(8,128)(2,1)S(1)} collective-permute-done((bf16[256,2,2,128]{3,0,1,2:T(8,128)(2,1)S(1)}, bf16[256,2,2,128]{3,0,1,2:T(8,128)(2,1)S(1)}, u32[]{:S(2)}, u32[]{:S(2)}) %collective-permute-start.5) | collective-permute-done | bytes 262176 | tf_op jit(solution)/shard_map/ppermute | solution.py:116
  61.1 1.4 collective-permute-start.6
  62.7 4.8 %collective-permute-done.6 = bf16[256,2,2,128]{3,0,1,2:T(8,128)(2,1)S(1)} collective-permute-done((bf16[256,2,2,128]{3,0,1,2:T(8,128)(2,1)S(1)}, bf16[256,2,2,128]{3,0,1,2:T(8,128)(2,1)S(1)}, u32[]{:S(2)}, u32[]{:S(2)}) %collective-permute-start.6) | collective-permute-done | bytes 262176 | tf_op jit(solution)/shard_map/ppermute | solution.py:116
  67.6 1.0 bitcast_dynamic-update-slice_fusion
  68.6 3.2 %gather_fusion.3 = bf16[16,256,2,2,128]{4,1,2,3,0:T(8,128)(2,1)} fusion(bf16[8,256,2,2,128]{4,1,2,3,0:T(8,128)(2,1)S(1)} %bitcast_dynamic-update-slice_fusion, s32[1024]{0:T(1024)} %pad_clamp_fusion), kind=kCustom, calls=%fused_computation.3 | custom fusion | bytes 8388672 | tf_op jit(solution)/shard_map/jit(_take)/gather | solution.py:197
  71.8 8.0 %fusion.2 = (f32[16,2,256,2]{2,3,1,0:T(2,128)S(1)}, f32[16,2,256,2,128]{2,4,3,1,0:T(8,128)}) fusion(pred[16,128]{1,0:T(8,128)(4,1)S(1)} %add_compare_fusion, bf16[16,128,2,128,1]{1,3,4,2,0:T(8,128)(2,1)} %bitcast.182, bf16[16,256,2,2,128]{4,1,2,3,0:T(8,128)(2,1)} %gather_fusion.3, pred[16]{0:T(512)(128)(4,1)S(1)} %copy-done.28), kind=kOutput, calls=%fused_computation.9 | convolution fusion | flops 545243136 | bytes 13699088 | tf_op jit(solution)/shard_map/bnkhc,bthc->bhnkt/dot_general | solution.py:201
  80.1 0.7 gather_fusion.4
  81.0 4.7 %fusion.3 = f32[16,2,256,2]{2,3,1,0:T(2,128)S(1)} fusion(f32[16,2,256,2,128]{2,4,3,1,0:T(8,128)} %get-tuple-element.62, f32[16,2,256,2]{2,3,1,0:T(2,128)S(1)} %broadcast_select_fusion, pred[16,128]{1,0:T(8,128)(4,1)S(1)} %add_compare_fusion), kind=kLoop, calls=%fused_computation.10 | loop fusion | flops 8372224 | bytes 8521728 | tf_op jit(solution)/shard_map/reduce_sum | solution.py:216
  85.7 5.2 %fusion.5 = f32[16,2,256,2,128]{4,2,3,1,0:T(8,128)S(1)} fusion(bf16[16,128,2,128,1]{1,3,4,2,0:T(8,128)(2,1)S(1)} %bitcast.172, f32[16,2,256,2,128]{2,4,3,1,0:T(8,128)} %get-tuple-element.62, f32[16,2,256,2]{2,3,1,0:T(2,128)S(1)} %broadcast_select_fusion, pred[16,128]{1,0:T(8,128)(4,1)S(1)} %add_compare_fusion), kind=kOutput, calls=%fused_computation.18 | convolution fusion | flops 545259520 | bytes 17893376 | tf_op jit(solution)/shard_map/bhnkt,bthc->bhnkc/dot_general | solution.py:217
  90.9 6.3 %fusion.23 = bf16[8,2,256,2,128]{4,0,3,2,1:T(8,128)(2,1)S(1)} fusion(f32[16,2,256,2,128]{4,2,3,1,0:T(8,128)S(1)} %fusion.5, s32[16]{0:T(128)S(1)} %copy-done.26), kind=kOutput, calls=%fused_computation.41 | convolution fusion | flops 202375296 | bytes 10485824 | tf_op jit(solution)/shard_map/rb,bhnkc->rhnkc/dot_general | solution.py:224
  97.7 1.0 copy.231
  99.0 8.3 %fusion.20 = bf16[8,1056,128]{2,1,0:T(8,128)(2,1)S(1)} fusion(s32[]{:T(128)S(6)} %select_n.195, bf16[8,1024,128]{2,1,0:T(8,128)(2,1)S(1)} %copy.232, bf16[8,32,128]{2,1,0:T(8,128)(2,1)S(1)} %copy.233), kind=kLoop, calls=%fused_computation.37 | loop fusion | flops 8650752 | bytes 4325380 | tf_op jit(solution)/shard_map/jit(_roll_dynamic)/concatenate | solution.py:240
  107.3 1.3 copy-done.3
  108.8 4.2 %collective-permute-start.7 = (bf16[1,1056,128]{2,1,0:T(8,128)(2,1)S(1)}, bf16[1,1056,128]{2,1,0:T(8,128)(2,1)S(1)}, u32[]{:S(2)}, u32[]{:S(2)}) collective-permute-start(bf16[1,1056,128]{2,1,0:T(8,128)(2,1)S(1)} %get-tuple-element.37), channel_id=1, source_target_pairs={{0,7},{1,0},{2,1},{3,2},{4,3},{5,4},{6,5},{7,6},{8,15},{9,8},{10,9... | collective-permute-start | bytes 811016 | tf_op jit(solution)/shard_map/ppermute | solution.py:246
  113.7 0.6 collective-permute-start.13
  114.3 0.9 collective-permute-start.12
  115.3 1.1 collective-permute-start.11
  116.4 3.6 %collective-permute-done.7 = bf16[1,1056,128]{2,1,0:T(8,128)(2,1)S(1)} collective-permute-done((bf16[1,1056,128]{2,1,0:T(8,128)(2,1)S(1)}, bf16[1,1056,128]{2,1,0:T(8,128)(2,1)S(1)}, u32[]{:S(2)}, u32[]{:S(2)}) %collective-permute-start.7) | collective-permute-done | bytes 270368 | tf_op jit(solution)/shard_map/ppermute | solution.py:246
  119.9 2.5 %collective-permute-start.9 = (bf16[1,1056,128]{2,1,0:T(8,128)(2,1)S(1)}, bf16[1,1056,128]{2,1,0:T(8,128)(2,1)S(1)}, u32[]{:S(2)}, u32[]{:S(2)}) collective-permute-start(bf16[1,1056,128]{2,1,0:T(8,128)(2,1)S(1)} %get-tuple-element.35), channel_id=1, source_target_pairs={{0,5},{1,6},{2,7},{3,0},{4,1},{5,2},{6,3},{7,4},{8,13},{9,14},{10,... | collective-permute-start | bytes 811016 | tf_op jit(solution)/shard_map/ppermute | solution.py:246
  122.4 9.0 %collective-permute-done.8 = bf16[1,1056,128]{2,1,0:T(8,128)(2,1)S(1)} collective-permute-done((bf16[1,1056,128]{2,1,0:T(8,128)(2,1)S(1)}, bf16[1,1056,128]{2,1,0:T(8,128)(2,1)S(1)}, u32[]{:S(2)}, u32[]{:S(2)}) %collective-permute-start.8) | collective-permute-done | bytes 270368 | tf_op jit(solution)/shard_map/ppermute | solution.py:246
  131.4 14.2 %collective-permute-start.10 = (bf16[1,1056,128]{2,1,0:T(8,128)(2,1)S(1)}, bf16[1,1056,128]{2,1,0:T(8,128)(2,1)S(1)}, u32[]{:S(2)}, u32[]{:S(2)}) collective-permute-start(bf16[1,1056,128]{2,1,0:T(8,128)(2,1)S(1)} %get-tuple-element.34), channel_id=1, source_target_pairs={{0,4},{1,5},{2,6},{3,7},{4,0},{5,1},{6,2},{7,3},{8,12},{9,13},{10,... | collective-permute-start | bytes 811016 | tf_op jit(solution)/shard_map/ppermute | solution.py:246
  145.8 10.2 %collective-permute-done.10 = bf16[1,1056,128]{2,1,0:T(8,128)(2,1)S(1)} collective-permute-done((bf16[1,1056,128]{2,1,0:T(8,128)(2,1)S(1)}, bf16[1,1056,128]{2,1,0:T(8,128)(2,1)S(1)}, u32[]{:S(2)}, u32[]{:S(2)}) %collective-permute-start.10) | collective-permute-done | bytes 270368 | tf_op jit(solution)/shard_map/ppermute | solution.py:246
  156.2 1.0 slice_dynamic-update-slice_fusion
  157.2 0.8 fusion.18
  158.0 1.3 copy-done.4
  160.0 0.6 fusion.129
  160.9 1.3 fusion.47
  162.6 3.1 %multiply_reduce_fusion = f32[1024,128]{1,0:T(8,128)S(1)} fusion(bf16[8,1056,128]{2,1,0:T(8,128)(2,1)} %copy-done.4, f32[8,1024]{1,0:T(8,128)S(1)} %subtract_exponential_fusion.2), kind=kLoop, calls=%fused_computation.19 | loop fusion | flops 3014656 | bytes 2654208 | tf_op jit(solution)/shard_map/reduce_sum | solution.py:264
  166.4 1.7 convolution_multiply_fusion.3
  168.2 1.9 fusion.16
  171.8 0.9 constant_dynamic-slice_fusion.2
  172.7 1.7 collective-permute-start.16
  174.4 7.1 %collective-permute-done.14 = bf16[64,2048]{1,0:T(8,128)(2,1)} collective-permute-done((bf16[64,2048]{1,0:T(8,128)(2,1)}, bf16[64,2048]{1,0:T(8,128)(2,1)}, u32[]{:S(2)}, u32[]{:S(2)}) %collective-permute-start.14) | collective-permute-done | bytes 262176 | tf_op jit(solution)/shard_map/ppermute | solution.py:102
  181.5 5.7 %collective-permute-done.15 = bf16[64,2048]{1,0:T(8,128)(2,1)} collective-permute-done((bf16[64,2048]{1,0:T(8,128)(2,1)S(1)}, bf16[64,2048]{1,0:T(8,128)(2,1)}, u32[]{:S(2)}, u32[]{:S(2)}) %collective-permute-start.15) | collective-permute-done | bytes 262176 | tf_op jit(solution)/shard_map/ppermute | solution.py:102
  187.2 1.9 fusion.53
  (143 shorter events, 13.6 us)
Async XLA Ops:
  6.5 23.4 %copy-start = (bf16[2,2048,256]{2,1,0:T(8,128)(2,1)S(1)}, bf16[2,2048,256]{2,1,0:T(8,128)(2,1)}, u32[]{:S(2)}) copy-start(bf16[2,2048,256]{2,1,0:T(8,128)(2,1)} %param.20) | copy-start | bytes 6291460
  6.5 8.3 %copy-start.2 = (s32[8]{0:T(128)S(1)}, s32[8]{0:T(128)}, u32[]{:S(2)}) copy-start(s32[8]{0:T(128)} %constant.144.clone) | copy-start | bytes 100
  6.5 9.6 %copy-start.13 = (s32[1,256,2]{1,2,0:T(2,128)S(1)}, s32[1,256,2]{1,2,0:T(2,128)}, u32[]{:S(2)}) copy-start(s32[1,256,2]{1,2,0:T(2,128)} %param.18) | copy-start | bytes 6148
  6.5 23.4 %all-gather.2.cloned.1.call-start = ((), (), s32[]{:S(2)}) async-start(), calls=%async_computation | async-start | bytes 1310720 | tf_op jit(solution)/shard_map/all_gather | solution.py:146
  12.8 5.7 %copy-start.15 = (s32[1024]{0:T(1024)}, s32[1024]{0:T(1024)S(1)}, u32[]{:S(2)}) copy-start(s32[1024]{0:T(1024)S(1)} %pad_clamp_fusion.1) | copy-start | bytes 12292
  25.1 7.9 %copy-start.25 = (s32[16]{0:T(128)}, s32[16]{0:T(128)S(1)}, u32[]{:S(2)}) copy-start(s32[16]{0:T(128)S(1)} %broadcast_add_fusion) | copy-start | bytes 196
  30.0 3.0 %copy-start.10 = (bf16[256,2048]{1,0:T(8,128)(2,1)S(1)}, bf16[256,2048]{1,0:T(8,128)(2,1)}, u32[]{:S(2)}) copy-start(bf16[256,2048]{1,0:T(8,128)(2,1)} %all-gather.2.cloned.1.call-done) | copy-start | bytes 3145732
  32.2 4.2 %copy-start.12 = (f32[2,256,256]{1,2,0:T(8,128)}, f32[2,256,256]{1,2,0:T(8,128)S(1)}, u32[]{:S(2)}) copy-start(f32[2,256,256]{1,2,0:T(8,128)S(1)} %convolution_bitcast_fusion) | copy-start | bytes 1572868
  36.8 0.9 copy-start.9
  37.0 3.0 %slice-start = ((f32[2,256,256]{1,2,0:T(8,128)}), f32[1,256,256]{1,2,0:T(8,128)S(1)}, s32[]{:S(2)}) async-start(f32[2,256,256]{1,2,0:T(8,128)} %copy-done.12), calls=%async_computation.1 | async-start | bytes 524288 | tf_op jit(solution)/shard_map/slice | solution.py:158
  37.8 3.9 %copy-start.6 = (bf16[256,2,2,64]{3,0,1,2:T(8,128)(2,1)}, bf16[256,2,2,64]{3,0,1,2:T(8,128)(2,1)S(1)}, u32[]{:S(2)}) copy-start(bf16[256,2,2,64]{3,0,1,2:T(8,128)(2,1)S(1)} %get-tuple-element.41) | copy-start | bytes 393220
  38.0 8.6 %collective-permute-start.3 = (bf16[256,2,2,128]{3,0,1,2:T(8,128)(2,1)S(1)}, bf16[256,2,2,128]{3,0,1,2:T(8,128)(2,1)}, u32[]{:S(2)}, u32[]{:S(2)}) collective-permute-start(bf16[256,2,2,128]{3,0,1,2:T(8,128)(2,1)S(1)} %pad_maximum_fusion), channel_id=1, source_target_pairs={{0,1},{1,3},{3,5},{5,7},{7,6},{6,4},{4,2},{2,0},{8,9},{9,11},{11,1... | collective-permute-start | bytes 786440 | tf_op jit(solution)/shard_map/ppermute | solution.py:116
  39.5 8.9 %collective-permute-start = (bf16[256,2,2,128]{3,0,1,2:T(8,128)(2,1)S(1)}, bf16[256,2,2,128]{3,0,1,2:T(8,128)(2,1)}, u32[]{:S(2)}, u32[]{:S(2)}) collective-permute-start(bf16[256,2,2,128]{3,0,1,2:T(8,128)(2,1)S(1)} %pad_maximum_fusion), channel_id=1, source_target_pairs={{1,0},{3,1},{5,3},{7,5},{6,7},{4,6},{2,4},{0,2},{9,8},{11,9},{13,1... | collective-permute-start | bytes 786440 | tf_op jit(solution)/shard_map/ppermute | solution.py:120
  40.3 7.7 %copy-start.11 = (bf16[256,2048]{1,0:T(8,128)(2,1)S(1)}, bf16[256,2048]{1,0:T(8,128)(2,1)}, u32[]{:S(2)}) copy-start(bf16[256,2048]{1,0:T(8,128)(2,1)} %all-gather.2.cloned.1.call-done) | copy-start | bytes 3145732
  40.4 7.7 %copy-start.14 = (bf16[2048,4]{0,1:T(4,128)(2,1)S(1)}, bf16[2048,4]{0,1:T(4,128)(2,1)}, u32[]{:S(2)}) copy-start(bf16[2048,4]{0,1:T(4,128)(2,1)} %param.17) | copy-start | bytes 49156
  41.7 14.1 %copy-start.7 = (bf16[256,2,2,64]{3,0,1,2:T(8,128)(2,1)S(1)}, bf16[256,2,2,64]{3,0,1,2:T(8,128)(2,1)}, u32[]{:S(2)}) copy-start(bf16[256,2,2,64]{3,0,1,2:T(8,128)(2,1)} %copy-done.6) | copy-start | bytes 393220
  46.6 7.8 %collective-permute-start.4 = (bf16[256,2,2,128]{3,0,1,2:T(8,128)(2,1)}, bf16[256,2,2,128]{3,0,1,2:T(8,128)(2,1)S(1)}, u32[]{:S(2)}, u32[]{:S(2)}) collective-permute-start(bf16[256,2,2,128]{3,0,1,2:T(8,128)(2,1)} %collective-permute-done.3), channel_id=1, source_target_pairs={{0,1},{1,3},{3,5},{5,7},{7,6},{6,4},{4,2},{2,0},{8,9},{9,11},{11,1... | collective-permute-start | bytes 786440 | tf_op jit(solution)/shard_map/ppermute | solution.py:116
  48.4 7.6 %collective-permute-start.1 = (bf16[256,2,2,128]{3,0,1,2:T(8,128)(2,1)}, bf16[256,2,2,128]{3,0,1,2:T(8,128)(2,1)S(1)}, u32[]{:S(2)}, u32[]{:S(2)}) collective-permute-start(bf16[256,2,2,128]{3,0,1,2:T(8,128)(2,1)} %collective-permute-done), channel_id=1, source_target_pairs={{1,0},{3,1},{5,3},{7,5},{6,7},{4,6},{2,4},{0,2},{9,8},{11,9},{13,1... | collective-permute-start | bytes 786440 | tf_op jit(solution)/shard_map/ppermute | solution.py:120
  54.4 6.7 %collective-permute-start.5 = (bf16[256,2,2,128]{3,0,1,2:T(8,128)(2,1)S(1)}, bf16[256,2,2,128]{3,0,1,2:T(8,128)(2,1)S(1)}, u32[]{:S(2)}, u32[]{:S(2)}) collective-permute-start(bf16[256,2,2,128]{3,0,1,2:T(8,128)(2,1)S(1)} %collective-permute-done.4), channel_id=1, source_target_pairs={{0,1},{1,3},{3,5},{5,7},{7,6},{6,4},{4,2},{2,0},{8,9},{9,11},{11,1... | collective-permute-start | bytes 786440 | tf_op jit(solution)/shard_map/ppermute | solution.py:116
  56.0 6.6 %collective-permute-start.2 = (bf16[256,2,2,128]{3,0,1,2:T(8,128)(2,1)S(1)}, bf16[256,2,2,128]{3,0,1,2:T(8,128)(2,1)S(1)}, u32[]{:S(2)}, u32[]{:S(2)}) collective-permute-start(bf16[256,2,2,128]{3,0,1,2:T(8,128)(2,1)S(1)} %collective-permute-done.1), channel_id=1, source_target_pairs={{1,0},{3,1},{5,3},{7,5},{6,7},{4,6},{2,4},{0,2},{9,8},{11,9},{13,1... | collective-permute-start | bytes 786440 | tf_op jit(solution)/shard_map/ppermute | solution.py:120
  61.1 6.4 %collective-permute-start.6 = (bf16[256,2,2,128]{3,0,1,2:T(8,128)(2,1)S(1)}, bf16[256,2,2,128]{3,0,1,2:T(8,128)(2,1)S(1)}, u32[]{:S(2)}, u32[]{:S(2)}) collective-permute-start(bf16[256,2,2,128]{3,0,1,2:T(8,128)(2,1)S(1)} %collective-permute-done.5), channel_id=1, source_target_pairs={{0,1},{1,3},{3,5},{5,7},{7,6},{6,4},{4,2},{2,0},{8,9},{9,11},{11,1... | collective-permute-start | bytes 786440 | tf_op jit(solution)/shard_map/ppermute | solution.py:116
  68.6 3.2 %copy-start.28 = (pred[16]{0:T(512)(128)(4,1)S(1)}, pred[16]{0:T(512)(128)(4,1)}, u32[]{:S(2)}) copy-start(pred[16]{0:T(512)(128)(4,1)} %get-tuple-element.64) | copy-start | bytes 52
  71.8 8.0 %copy-start.27 = (pred[8,16]{1,0:T(8,128)(4,1)S(1)}, pred[8,16]{1,0:T(8,128)(4,1)}, u32[]{:S(2)}) copy-start(pred[8,16]{1,0:T(8,128)(4,1)} %iota_compare_fusion.2) | copy-start | bytes 388
  80.1 0.8 copy-start.20
  85.7 5.2 %copy-start.26 = (s32[16]{0:T(128)S(1)}, s32[16]{0:T(128)}, u32[]{:S(2)}) copy-start(s32[16]{0:T(128)} %copy-done.25) | copy-start | bytes 196
  107.3 1.4 copy-start.3
  108.8 11.2 %collective-permute-start.7 = (bf16[1,1056,128]{2,1,0:T(8,128)(2,1)S(1)}, bf16[1,1056,128]{2,1,0:T(8,128)(2,1)S(1)}, u32[]{:S(2)}, u32[]{:S(2)}) collective-permute-start(bf16[1,1056,128]{2,1,0:T(8,128)(2,1)S(1)} %get-tuple-element.37), channel_id=1, source_target_pairs={{0,7},{1,0},{2,1},{3,2},{4,3},{5,4},{6,5},{7,6},{8,15},{9,8},{10,9... | collective-permute-start | bytes 811016 | tf_op jit(solution)/shard_map/ppermute | solution.py:246
  113.1 18.4 %collective-permute-start.8 = (bf16[1,1056,128]{2,1,0:T(8,128)(2,1)S(1)}, bf16[1,1056,128]{2,1,0:T(8,128)(2,1)S(1)}, u32[]{:S(2)}, u32[]{:S(2)}) collective-permute-start(bf16[1,1056,128]{2,1,0:T(8,128)(2,1)S(1)} %get-tuple-element.36), channel_id=1, source_target_pairs={{0,6},{1,7},{2,0},{3,1},{4,2},{5,3},{6,4},{7,5},{8,14},{9,15},{10,... | collective-permute-start | bytes 811016 | tf_op jit(solution)/shard_map/ppermute | solution.py:246
  113.7 42.5 %collective-permute-start.13 = (bf16[1,1056,128]{2,1,0:T(8,128)(2,1)S(1)}, bf16[1,1056,128]{2,1,0:T(8,128)(2,1)S(1)}, u32[]{:S(2)}, u32[]{:S(2)}) collective-permute-start(bf16[1,1056,128]{2,1,0:T(8,128)(2,1)S(1)} %get-tuple-element.31), channel_id=1, source_target_pairs={{0,1},{1,2},{2,3},{3,4},{4,5},{5,6},{6,7},{7,0},{8,9},{9,10},{10,1... | collective-permute-start | bytes 811016 | tf_op jit(solution)/shard_map/ppermute | solution.py:246
  114.3 41.8 %collective-permute-start.12 = (bf16[1,1056,128]{2,1,0:T(8,128)(2,1)S(1)}, bf16[1,1056,128]{2,1,0:T(8,128)(2,1)S(1)}, u32[]{:S(2)}, u32[]{:S(2)}) collective-permute-start(bf16[1,1056,128]{2,1,0:T(8,128)(2,1)S(1)} %get-tuple-element.32), channel_id=1, source_target_pairs={{0,2},{1,3},{2,4},{3,5},{4,6},{5,7},{6,0},{7,1},{8,10},{9,11},{10,... | collective-permute-start | bytes 811016 | tf_op jit(solution)/shard_map/ppermute | solution.py:246
  115.3 40.8 %collective-permute-start.11 = (bf16[1,1056,128]{2,1,0:T(8,128)(2,1)S(1)}, bf16[1,1056,128]{2,1,0:T(8,128)(2,1)S(1)}, u32[]{:S(2)}, u32[]{:S(2)}) collective-permute-start(bf16[1,1056,128]{2,1,0:T(8,128)(2,1)S(1)} %get-tuple-element.33), channel_id=1, source_target_pairs={{0,3},{1,4},{2,5},{3,6},{4,7},{5,0},{6,1},{7,2},{8,11},{9,12},{10,... | collective-permute-start | bytes 811016 | tf_op jit(solution)/shard_map/ppermute | solution.py:246
  119.9 25.8 %collective-permute-start.9 = (bf16[1,1056,128]{2,1,0:T(8,128)(2,1)S(1)}, bf16[1,1056,128]{2,1,0:T(8,128)(2,1)S(1)}, u32[]{:S(2)}, u32[]{:S(2)}) collective-permute-start(bf16[1,1056,128]{2,1,0:T(8,128)(2,1)S(1)} %get-tuple-element.35), channel_id=1, source_target_pairs={{0,5},{1,6},{2,7},{3,0},{4,1},{5,2},{6,3},{7,4},{8,13},{9,14},{10,... | collective-permute-start | bytes 811016 | tf_op jit(solution)/shard_map/ppermute | solution.py:246
  131.4 24.6 %collective-permute-start.10 = (bf16[1,1056,128]{2,1,0:T(8,128)(2,1)S(1)}, bf16[1,1056,128]{2,1,0:T(8,128)(2,1)S(1)}, u32[]{:S(2)}, u32[]{:S(2)}) collective-permute-start(bf16[1,1056,128]{2,1,0:T(8,128)(2,1)S(1)} %get-tuple-element.34), channel_id=1, source_target_pairs={{0,4},{1,5},{2,6},{3,7},{4,0},{5,1},{6,2},{7,3},{8,12},{9,13},{10,... | collective-permute-start | bytes 811016 | tf_op jit(solution)/shard_map/ppermute | solution.py:246
  158.0 1.4 copy-start.4
  162.2 3.5 %copy-start.8 = (f32[2,256,2,128]{3,1,2,0:T(8,128)S(1)}, f32[2,256,2,128]{3,1,2,0:T(8,128)}, u32[]{:S(2)}) copy-start(f32[2,256,2,128]{3,1,2,0:T(8,128)} %fusion.43) | copy-start | bytes 1572868
  162.6 3.9 %copy-start.21 = (pred[256]{0:T(512)(128)(4,1)S(1)}, pred[256]{0:T(512)(128)(4,1)}, u32[]{:S(2)}) copy-start(pred[256]{0:T(512)(128)(4,1)} %get-tuple-element.24) | copy-start | bytes 772
  162.6 3.9 %copy-start.22 = (pred[256]{0:T(512)(128)(4,1)S(1)}, pred[256]{0:T(512)(128)(4,1)}, u32[]{:S(2)}) copy-start(pred[256]{0:T(512)(128)(4,1)} %get-tuple-element.25) | copy-start | bytes 772
  166.3 1.9 copy-start.18
  166.3 1.9 copy-start.19
  168.2 2.5 %copy-start.5 = (bf16[4,256,2048]{2,1,0:T(8,128)(2,1)S(1)}, bf16[4,256,2048]{2,1,0:T(8,128)(2,1)}, u32[]{:S(2)}) copy-start(bf16[4,256,2048]{2,1,0:T(8,128)(2,1)} %param.21) | copy-start | bytes 12582916
  168.2 2.5 %copy-start.16 = (pred[256]{0:T(512)(128)(4,1)S(1)}, pred[256]{0:T(512)(128)(4,1)}, u32[]{:S(2)}) copy-start(pred[256]{0:T(512)(128)(4,1)} %get-tuple-element.20) | copy-start | bytes 772
  168.2 2.5 %copy-start.17 = (pred[256]{0:T(512)(128)(4,1)S(1)}, pred[256]{0:T(512)(128)(4,1)}, u32[]{:S(2)}) copy-start(pred[256]{0:T(512)(128)(4,1)} %get-tuple-element.22) | copy-start | bytes 772
  170.7 0.6 copy-start.23
  170.7 0.7 copy-start.24
  171.3 17.8 %copy-start.1 = (bf16[2,2048,256]{2,1,0:T(8,128)(2,1)S(1)}, bf16[2,2048,256]{2,1,0:T(8,128)(2,1)}, u32[]{:S(2)}) copy-start(bf16[2,2048,256]{2,1,0:T(8,128)(2,1)} %param.20) | copy-start | bytes 6291460
  172.7 8.9 %collective-permute-start.14 = (bf16[64,2048]{1,0:T(8,128)(2,1)}, bf16[64,2048]{1,0:T(8,128)(2,1)}, u32[]{:S(2)}, u32[]{:S(2)}) collective-permute-start(bf16[64,2048]{1,0:T(8,128)(2,1)} %get-tuple-element.42), channel_id=1, source_target_pairs={{0,8},{8,16},{16,24},{24,0},{1,9},{9,17},{17,25},{25,1},{2,10},{10... | collective-permute-start | bytes 786440 | tf_op jit(solution)/shard_map/ppermute | solution.py:102
  172.7 8.9 %collective-permute-start.16 = (bf16[64,2048]{1,0:T(8,128)(2,1)}, bf16[64,2048]{1,0:T(8,128)(2,1)}, u32[]{:S(2)}, u32[]{:S(2)}) collective-permute-start(bf16[64,2048]{1,0:T(8,128)(2,1)} %get-tuple-element.43), channel_id=1, source_target_pairs={{0,24},{8,0},{16,8},{24,16},{1,25},{9,1},{17,9},{25,17},{2,26},{10... | collective-permute-start | bytes 786440 | tf_op jit(solution)/shard_map/ppermute | solution.py:102
  174.4 12.8 %collective-permute-start.15 = (bf16[64,2048]{1,0:T(8,128)(2,1)S(1)}, bf16[64,2048]{1,0:T(8,128)(2,1)}, u32[]{:S(2)}, u32[]{:S(2)}) collective-permute-start(bf16[64,2048]{1,0:T(8,128)(2,1)S(1)} %get-tuple-element.44), channel_id=1, source_target_pairs={{0,16},{8,24},{16,0},{24,8},{1,17},{9,25},{17,1},{25,9},{2,18},{10... | collective-permute-start | bytes 786440 | tf_op jit(solution)/shard_map/ppermute | solution.py:102
Sparse Core Ops, SparseCore 0:
  10.4 19.4 all-gather.1
